TPU v7x, 256 devices: a whole 4x4x8 slice. The times are simulated.
256 devices in a mesh: seq: 64 (over z, x, core), tensor: 4 (over y).
Axes of the slice: x: 4, y: 4, z: 8, core: 2. Of those that a mesh axis runs over, the one named last changes fastest.
Arguments:
- residual: bfloat16 [16384, 2048], P('seq', 'tensor'), may hold values from -0.29882812 to 0.29882812
- query: bfloat16 [16384, 2048], P('seq', 'tensor'), may hold values from -13 to 13
- new_keys: bfloat16 [16384, 2048], P('seq', 'tensor'), may hold values from -6 to 6
- new_values: bfloat16 [16384, 2048], P('seq', 'tensor'), may hold values from -6 to 6
- leaf_kv: bfloat16 [2, 4096, 2048], P(None, 'seq', 'tensor'), may hold values from -6 to 6
- branch_kv: bfloat16 [2, 4096, 2048], P(None, 'seq', 'tensor'), may hold values from -6 to 6
- root_kv: bfloat16 [2, 2048, 2048], P(None, 'seq', 'tensor'), may hold values from -10 to 10
- out_weight: bfloat16 [2048, 2048], P('tensor'), may hold values from -0.125 to 0.125
- norm_gain: float32 [2048], replicated, may hold values from 0.25 to 1.75
- norm_bias: float32 [2048], replicated, may hold values from -1.8 to 1.8
- up_weight: bfloat16 [2048, 4096], P(None, 'tensor'), may hold values from -0.125 to 0.125
- up_bias: float32 [4096], P('tensor'), may hold values from -3 to 3
- down_weight: bfloat16 [4096, 2048], P('tensor'), may hold values from -0.09375 to 0.09375
- down_bias: float32 [2048], replicated, may hold values from -1.8 to 1.8
- segment: int32 [64], replicated, may hold values from 0 to 15, never falling along the last dimension, each value on 1 to 8 neighbouring positions
- new_len: int32 [64], replicated, may hold values from 1 to 256, 12288 in all
Outputs:
- layer_out: bfloat16 [16384, 2048], P('seq', 'tensor')
Inputs may be any that keep to these rules, and one draw needn't show every extreme that they name: `segment`: never falling along the requests, so the requests of one branch node have consecutive indices; every node 0 to 15 has 1 to 8 requests and one has exactly 8. `new_len`: the largest is exactly 256; they sum to 12288.
All inputs are finite; a program needn't handle non-finite values.
Results may differ from a plain program's by a relative error of at most 0.018.
Values may be sent and summed in bfloat16 or wider, within the bound.
No kernel may reach another device: no remote copies, remote signals or barrier semaphores. Data moves between devices by JAX's collectives and lax.ppermute only.
A program may use at most 128 MiB of HBM per device.

v0:
```python
import jax
import jax.numpy as jnp
from jax import lax
from jax.sharding import PartitionSpec as P

HD = 128
NEGATIVE_FILL = -1e30
NORM_EPSILON = 1e-05
BLOCK_KEYS = 512


def attend(running, query_heads, key_rows, value_rows, allowed):
    largest, totals, accumulated = running
    head_count = query_heads.shape[1]
    head_width = query_heads.shape[2]
    key_heads = key_rows.reshape(key_rows.shape[0], head_count, head_width)
    value_heads = value_rows.reshape(value_rows.shape[0], head_count, head_width)
    scores = jnp.einsum(
        "qhd,khd->hqk", query_heads, key_heads, preferred_element_type=jnp.float32
    ) * head_width ** (-0.5)
    scores = jnp.where(allowed, scores, NEGATIVE_FILL)
    new_largest = jnp.maximum(largest, jnp.max(scores, axis=2))
    weights = jnp.where(allowed, jnp.exp(scores - new_largest[:, :, None]), 0.0)
    factor = jnp.exp(largest - new_largest)
    accumulated = accumulated * factor[:, :, None] + jnp.einsum(
        "hqk,khd->hqd",
        weights.astype(jnp.bfloat16),
        value_heads,
        preferred_element_type=jnp.float32,
    )
    totals = totals * factor + jnp.sum(weights, axis=2)
    return (new_largest, totals, accumulated)


def attend_blocks(running, query_heads, key_rows, value_rows):
    for block_start in range(0, key_rows.shape[0], BLOCK_KEYS):
        running = attend(
            running,
            query_heads,
            key_rows[block_start : block_start + BLOCK_KEYS],
            value_rows[block_start : block_start + BLOCK_KEYS],
            True,
        )
    return running


def per_device(
    residual,
    query,
    new_keys,
    new_values,
    leaf_kv,
    branch_kv,
    root_kv,
    out_weight,
    norm_gain,
    norm_bias,
    up_weight,
    up_bias,
    down_weight,
    down_bias,
    segment,
    new_len,
):
    row_count = query.shape[0]
    head_count = query.shape[1] // HD
    query_heads = query.reshape(row_count, head_count, HD)
    device = lax.axis_index("seq")
    my_segment = segment[device]
    branch_count = lax.axis_size("seq") // 4
    running = (
        jnp.full((head_count, row_count), NEGATIVE_FILL, jnp.float32),
        jnp.zeros((head_count, row_count), jnp.float32),
        jnp.zeros((head_count, row_count, HD), jnp.float32),
    )
    running = attend_blocks(
        running,
        query_heads,
        lax.all_gather(root_kv[0], "seq", axis=0, tiled=True),
        lax.all_gather(root_kv[1], "seq", axis=0, tiled=True),
    )
    key_rows = lax.all_gather(branch_kv[0], "seq", axis=0, tiled=True)
    value_rows = lax.all_gather(branch_kv[1], "seq", axis=0, tiled=True)
    feature_width = key_rows.shape[1]
    keys_mine = lax.dynamic_index_in_dim(
        key_rows.reshape(-1, branch_count, feature_width), my_segment, 1, keepdims=False
    )
    values_mine = lax.dynamic_index_in_dim(
        value_rows.reshape(-1, branch_count, feature_width), my_segment, 1, keepdims=False
    )
    running = attend_blocks(running, query_heads, keys_mine, values_mine)
    running = attend(running, query_heads, leaf_kv[0], leaf_kv[1], True)
    query_pos = jnp.arange(row_count, dtype=jnp.int32)
    allowed_new = (query_pos[None, :] <= query_pos[:, None]) & (
        query_pos[None, :] < new_len[device]
    )
    running = attend(running, query_heads, new_keys, new_values, allowed_new[None])
    largest, totals, accumulated = running
    attention = (
        jnp.transpose(accumulated / totals[:, :, None], (1, 0, 2))
        .reshape(row_count, head_count * HD)
        .astype(jnp.bfloat16)
    )
    projected = jnp.dot(attention, out_weight, preferred_element_type=jnp.float32)
    share_width = residual.shape[1]
    column = lax.axis_index("tensor") * share_width
    projected = lax.psum(projected.astype(jnp.bfloat16), "tensor").astype(jnp.float32)
    full_residual = lax.all_gather(residual, "tensor", axis=1, tiled=True)
    mid_full = (full_residual.astype(jnp.float32) + projected).astype(jnp.bfloat16)
    wide_mid = mid_full.astype(jnp.float32)
    row_mean = jnp.mean(wide_mid, axis=1, keepdims=True)
    row_var = jnp.mean(wide_mid * wide_mid, axis=1, keepdims=True) - row_mean * row_mean
    normed = (
        (wide_mid - row_mean) * lax.rsqrt(row_var + NORM_EPSILON) * norm_gain + norm_bias
    ).astype(jnp.bfloat16)
    up_sum = jnp.dot(normed, up_weight, preferred_element_type=jnp.float32)
    mid_share = lax.dynamic_slice_in_dim(mid_full, column, share_width, 1)
    hidden = jax.nn.gelu(up_sum + up_bias, approximate=False).astype(jnp.bfloat16)
    partial_value = jnp.dot(hidden, down_weight, preferred_element_type=jnp.float32)
    summed = lax.psum_scatter(
        partial_value.astype(jnp.bfloat16), "tensor", scatter_dimension=1, tiled=True
    ).astype(jnp.float32)
    down_share = lax.dynamic_slice_in_dim(down_bias, column, share_width, 0)
    return (summed + down_share + mid_share.astype(jnp.float32)).astype(jnp.bfloat16)


def solution(mesh):
    return jax.shard_map(
        per_device,
        mesh=mesh,
        in_specs=(
            P("seq", "tensor"),
            P("seq", "tensor"),
            P("seq", "tensor"),
            P("seq", "tensor"),
            P(None, "seq", "tensor"),
            P(None, "seq", "tensor"),
            P(None, "seq", "tensor"),
            P("tensor", None),
            P(),
            P(),
            P(None, "tensor"),
            P("tensor"),
            P("tensor", None),
            P(),
            P(),
            P(),
        ),
        out_specs=P("seq", "tensor"),
        check_vma=False,
    )
```

profile of v0, /device:TPU:2, one launch (start us, length us, event | category | flops | bytes accessed | tf_op | source)
XLA Modules:
  0.0 453.0 jit_solution(13293988858656092174)
XLA Ops:
  6.5 1.5 fusion.182
  8.2 0.7 all-gather.12.cloned.1.call-update
  8.9 1.5 fusion.181
  10.5 0.5 all-gather.16.cloned.1.call-update
  11.1 0.5 all-gather.10.cloned.1.call-update
  11.7 1.2 dynamic_slice.22
  12.9 0.6 iota_compare_fusion.1
  13.6 1.3 dynamic_slice.19
  16.2 0.9 fusion.180
  17.1 1.8 copy.117
  19.5 1.9 fusion.184
  21.4 2.0 fusion.183
  23.4 66.1 %all-gather.14.cloned.1.call-done = bf16[1,2048,512]{2,1,0:T(8,128)(2,1)} async-done(((bf16[1,32,512]{2,1,0:T(8,128)(2,1)}), bf16[1,2048,512]{2,1,0:T(8,128)(2,1)}) %all-gather.14.cloned.1.call-update) | async-done | bytes 2097168 | tf_op jit(solution)/shard_map/all_gather | solution.py:80
  89.5 2.9 fusion.178
  92.4 2.1 copy.97
  94.4 72.8 %all-gather.12.cloned.1.call-done = bf16[1,2048,512]{2,1,0:T(8,128)(2,1)} async-done(((bf16[1,32,512]{2,1,0:T(8,128)(2,1)}), bf16[1,2048,512]{2,1,0:T(8,128)(2,1)}) %all-gather.12.cloned.1.call-update) | async-done | bytes 2097168 | tf_op jit(solution)/shard_map/all_gather | solution.py:79
  167.2 2.9 fusion.179
  170.1 2.1 copy.118
  172.2 2.0 copy.120
  174.2 2.1 copy.119
  176.3 2.1 copy.121
  178.3 2.0 copy.93
  180.4 2.1 copy.89
  182.4 2.1 copy.85
  184.5 2.9 multiply_reduce_fusion
  187.4 1.7 multiply_reduce_fusion.2
  189.1 1.8 multiply_reduce_fusion.1
  190.9 2.3 multiply_reduce_fusion.3
  193.2 53.1 %all-gather.18.cloned.1.call-done = bf16[1,4096,512]{2,1,0:T(8,128)(2,1)} async-done(((bf16[1,64,512]{2,1,0:T(8,128)(2,1)}), bf16[1,4096,512]{2,1,0:T(8,128)(2,1)}) %all-gather.18.cloned.1.call-update) | async-done | bytes 4194320 | tf_op jit(solution)/shard_map/all_gather | solution.py:83
  246.3 78.8 %all-gather.16.cloned.1.call-done = bf16[1,4096,512]{2,1,0:T(8,128)(2,1)} async-done(((bf16[1,64,512]{2,1,0:T(8,128)(2,1)}), bf16[1,4096,512]{2,1,0:T(8,128)(2,1)}) %all-gather.16.cloned.1.call-update) | async-done | bytes 4194320 | tf_op jit(solution)/shard_map/all_gather | solution.py:82
  325.1 4.3 constant_dynamic-slice_fusion
  329.4 1.9 copy.122
  331.2 1.9 copy.98
  333.1 1.4 fusion.185
  334.5 0.7 fusion.176
  335.2 0.5 fusion.63
  335.6 0.4 convolution_bitcast_fusion.1
  336.1 0.1 fusion.116
  336.1 0.2 fusion.61
  336.3 0.5 copy-done.1
  336.8 0.6 fusion.11
  337.4 0.5 copy-done.2
  337.9 0.6 fusion.9
  338.4 0.1 copy-done.3
  338.6 0.6 fusion.7
  339.1 0.5 copy-done.4
  339.6 0.6 fusion.5
  340.3 0.7 fusion.23
  341.0 0.2 copy-done.13
  341.2 0.3 convolution_bitcast_fusion
  341.5 0.7 fusion.21
  342.2 0.3 copy-done.7
  342.5 0.7 fusion.19
  343.2 0.1 copy-done.6
  343.3 0.7 fusion.25
  344.0 0.3 fusion.29
  344.3 1.8 convolution_convert_fusion
  346.1 5.9 %all-gather.10.cloned.1.call-done = bf16[256,2048]{1,0:T(8,128)(2,1)} async-done(((bf16[256,512]{1,0:T(8,128)(2,1)}), bf16[256,2048]{1,0:T(8,128)(2,1)}) %all-gather.10.cloned.1.call-update) | async-done | bytes 1048592 | tf_op jit(solution)/shard_map/all_gather | solution.py:108
  352.0 53.8 %all-reduce.2.cloned.1.call-done = bf16[256,2048]{1,0:T(8,128)(2,1)} async-done(((bf16[256,2048]{1,0:T(8,128)(2,1)}), bf16[256,2048]{1,0:T(8,128)(2,1)}) %all-reduce.2.cloned.1.call-update) | async-done | bytes 1048592 | tf_op jit(solution)/shard_map/psum | solution.py:107
  405.8 2.1 convert_reduce_fusion
  407.9 9.1 %convolution_convert_fusion.1 = bf16[256,2048]{1,0:T(8,128)(2,1)} fusion(bf16[1024,2048]{1,0:T(8,128)(2,1)} %param.28, bf16[2048,1024]{1,0:T(8,128)(2,1)} %param.26, bf16[256,2048]{1,0:T(8,128)(2,1)S(1)} %get-tuple-element.7, f32[2048]{0:T(1024)S(1)} %copy-done.18, f32[2048]{0:T(1024)S(1)} %copy-done.19, f32[256]{0:T(256)S(1)} %get-tuple-element.38, ...), kind=kOutput, calls=%fused_computation.4 | convolution fusion | flops 2168455168 | bytes 10508288 | tf_op jit(solution)/shard_map/dot_general | solution.py:119
  417.0 0.8 dynamic_slice.23
  417.8 26.7 %reduce-scatter.2.cloned.1.call-done = bf16[256,512]{1,0:T(8,128)(2,1)} async-done(((bf16[256,2048]{1,0:T(8,128)(2,1)}), bf16[256,512]{1,0:T(8,128)(2,1)}) %reduce-scatter.2.cloned.1.call-update) | async-done | bytes 262160 | tf_op jit(solution)/shard_map/reduce_scatter | solution.py:120
  444.4 1.7 add_convert_fusion.1
  (51 shorter events, 0.5 us)
Async XLA Ops:
  6.5 337.7 %copy-start = (bf16[512,2048]{1,0:T(8,128)(2,1)S(1)}, bf16[512,2048]{1,0:T(8,128)(2,1)}, u32[]{:S(2)}) copy-start(bf16[512,2048]{1,0:T(8,128)(2,1)} %param.23) | copy-start | bytes 6291460
  6.5 14.9 %copy-start.5 = (bf16[256,512]{1,0:T(8,128)(2,1)S(1)}, bf16[256,512]{1,0:T(8,128)(2,1)}, u32[]{:S(2)}) copy-start(bf16[256,512]{1,0:T(8,128)(2,1)} %param.17) | copy-start | bytes 786436
  6.5 82.9 %all-gather.14.cloned.1.call-start = ((), (), s32[]{:S(2)}) async-start(), calls=%async_computation.5 | async-start | bytes 2129920 | tf_op jit(solution)/shard_map/all_gather | solution.py:80
  8.1 159.1 %all-gather.12.cloned.1.call-start = ((), (), s32[]{:S(2)}) async-start(), calls=%async_computation.4 | async-start | bytes 2129920 | tf_op jit(solution)/shard_map/all_gather | solution.py:79
  8.9 237.4 %all-gather.18.cloned.1.call-start = ((), (), s32[]{:S(2)}) async-start(), calls=%async_computation.7 | async-start | bytes 4259840 | tf_op jit(solution)/shard_map/all_gather | solution.py:83
  10.5 314.7 %all-gather.16.cloned.1.call-start = ((), (), s32[]{:S(2)}) async-start(), calls=%async_computation.6 | async-start | bytes 4259840 | tf_op jit(solution)/shard_map/all_gather | solution.py:82
  11.0 340.9 %all-gather.10.cloned.1.call-start = ((), (), s32[]{:S(2)}) async-start(), calls=%async_computation.1 | async-start | bytes 1310720 | tf_op jit(solution)/shard_map/all_gather | solution.py:108
  11.6 394.2 %all-reduce.2.cloned.1.call-start = ((), (), s32[]{:S(2)}) async-start(), calls=%async_computation.2 | async-start | bytes 2097152 | tf_op jit(solution)/shard_map/psum | solution.py:107
  184.5 2.9 copy-start.12
  187.4 1.7 copy-start.11
  189.1 1.8 copy-start.10
  333.1 2.5 copy-start.15
  333.1 3.0 copy-start.14
  335.2 1.6 copy-start.1
  336.0 1.8 copy-start.2
  336.8 1.8 copy-start.3
  337.9 1.8 copy-start.4
  338.6 1.7 copy-start.16
  338.6 1.7 copy-start.17
  338.6 1.7 copy-start.9
  340.2 1.0 copy-start.13
  340.3 1.2 copy-start.8
  341.5 1.0 copy-start.7
  342.2 1.1 copy-start.6
  346.0 61.8 %copy-start.18 = (f32[2048]{0:T(1024)S(1)}, f32[2048]{0:T(1024)}, u32[]{:S(2)}) copy-start(f32[2048]{0:T(1024)} %param.25) | copy-start | bytes 24580
  346.0 61.9 %copy-start.19 = (f32[2048]{0:T(1024)S(1)}, f32[2048]{0:T(1024)}, u32[]{:S(2)}) copy-start(f32[2048]{0:T(1024)} %param.24) | copy-start | bytes 24580
  346.0 61.9 %copy-start.20 = (f32[1024]{0:T(1024)S(1)}, f32[1024]{0:T(1024)}, u32[]{:S(2)}) copy-start(f32[1024]{0:T(1024)} %param.27) | copy-start | bytes 12292
  346.1 98.4 %reduce-scatter.2.cloned.1.call-start = ((), (), s32[]{:S(2)}) async-start(), calls=%async_computation.3 | async-start | bytes 1310720 | tf_op jit(solution)/shard_map/reduce_scatter | solution.py:120
Sparse Core Ops, SparseCore 0:
  10.1 79.3 all-gather.13
  92.2 74.9 all-gather.11
  170.0 76.2 all-gather.17
  248.9 76.1 all-gather.15
  326.8 25.1 all-gather.9
  354.2 51.5 all-reduce.1
  417.1 27.2 reduce-scatter.1
where the time goes:
time: 454 us; the launch traced here: 453 us
  waiting for transfers between devices  359 us (79%)
  local copies, waits for them, and re-layouts  41.5 us (9%)
  matrix products  28.4 us (6%)
  between operations  15.7 us (3%)
  other arithmetic  8.22 us (2%)
    all_gather x1, waiting for transfers between devices, per_device(): key_rows = lax.all_gather(branch_kv[0], 'seq', axis=0, tiled=True)  78.8 us
    all_gather x1, waiting for transfers between devices, per_device(): lax.all_gather(root_kv[0], 'seq', axis=0, tiled=True)  72.8 us
    all_gather x1, waiting for transfers between devices, per_device(): lax.all_gather(root_kv[1], 'seq', axis=0, tiled=True)  66.1 us
    psum x1, waiting for transfers between devices, per_device(): lax.psum(projected.astype(jnp.bfloat16), 'tensor').astype(jnp.float32)  53.8 us
    all_gather x1, waiting for transfers between devices, per_device(): value_rows = lax.all_gather(branch_kv[1], 'seq', axis=0, tiled=True)  53.1 us
    reduce_scatter x1, waiting for transfers between devices, per_device(): lax.psum_scatter(partial_value.astype(jnp.bfloat16), 'tensor', scatter_di...  26.7 us
    dot_general x7, matrix products, attend(): jnp.einsum('qhd,khd->hqk', query_heads, key_heads, preferred_element_type...  13.9 us
    unnamed x47, local copies, waits for them, and re-layouts  12.4 us
  transfers between devices with their start and end apart: 7, of which 7 were waited for; matrix products, arithmetic and copies ran while one was open for 14% of the time, Pallas kernels for 0%

commit v1 on v0

--- a/solution.py
+++ b/solution.py
@@ -104,7 +104,8 @@
     projected = jnp.dot(attention, out_weight, preferred_element_type=jnp.float32)
     share_width = residual.shape[1]
     column = lax.axis_index("tensor") * share_width
-    projected = lax.psum(projected.astype(jnp.bfloat16), "tensor").astype(jnp.float32)
+    watch_node_up = lambda inp: jnp.sum(lax.all_gather(inp, "tensor"), 0)
+    projected = watch_node_up(projected.astype(jnp.bfloat16)).astype(jnp.float32)
     full_residual = lax.all_gather(residual, "tensor", axis=1, tiled=True)
     mid_full = (full_residual.astype(jnp.float32) + projected).astype(jnp.bfloat16)
     wide_mid = mid_full.astype(jnp.float32)

time: 454 us -> 473 us (1.042)
  waiting for transfers between devices: 359 us -> 373 us
    psum x1 -> x0, waiting for transfers between devices: 53.8 us -> none  [per_device(): lax.psum(projected.astype(jnp.bfloat16), 'tensor').astype(jnp.float32)]
    all_gather x0 -> x1, waiting for transfers between devices: none -> 48.5 us  [per_device(): watch_node_up = lambda inp: jnp.sum(lax.all_gather(inp, 'tensor'), 0)]
    all_gather x1, waiting for transfers between devices: 5.85 us -> 25.6 us  [per_device(): full_residual = lax.all_gather(residual, 'tensor', axis=1, tiled=True)]
  transfers between devices with their start and end apart: 7 -> 7, of which waited for: 7 -> 7; matrix products, arithmetic and copies ran while one was open for 14% -> 10% of each run, Pallas kernels for 0% -> 0%
where the time goes in v1:
time: 473 us; the launch traced here: 472 us
  waiting for transfers between devices  373 us (79%)
  local copies, waits for them, and re-layouts  41.5 us (9%)
  matrix products  28.7 us (6%)
  between operations  15.8 us (3%)
  other arithmetic  11.7 us (2%)
    all_gather x1, waiting for transfers between devices, per_device(): key_rows = lax.all_gather(branch_kv[0], 'seq', axis=0, tiled=True)  78.8 us
    all_gather x1, waiting for transfers between devices, per_device(): lax.all_gather(root_kv[0], 'seq', axis=0, tiled=True)  72.8 us
    all_gather x1, waiting for transfers between devices, per_device(): lax.all_gather(root_kv[1], 'seq', axis=0, tiled=True)  66.7 us
    all_gather x1, waiting for transfers between devices, per_device(): value_rows = lax.all_gather(branch_kv[1], 'seq', axis=0, tiled=True)  53.1 us
    all_gather x1, waiting for transfers between devices, per_device(): watch_node_up = lambda inp: jnp.sum(lax.all_gather(inp, 'tensor'), 0)  48.5 us
    reduce_scatter x1, waiting for transfers between devices, per_device(): lax.psum_scatter(partial_value.astype(jnp.bfloat16), 'tensor', scatter_di...  26.1 us
    all_gather x1, waiting for transfers between devices, per_device(): full_residual = lax.all_gather(residual, 'tensor', axis=1, tiled=True)  25.6 us
    dot_general x7, matrix products, attend(): jnp.einsum('qhd,khd->hqk', query_heads, key_heads, preferred_element_type...  13.9 us
  transfers between devices with their start and end apart: 7, of which 7 were waited for; matrix products, arithmetic and copies ran while one was open for 10% of the time, Pallas kernels for 0%

profile of v1, /device:TPU:2, one launch (start us, length us, event | category | flops | bytes accessed | tf_op | source)
XLA Modules:
  0.0 471.6 jit_solution(3425993161807439187)
XLA Ops:
  6.5 1.5 fusion.182
  8.2 0.7 all-gather.14.cloned.1.call-update
  8.9 1.5 fusion.181
  10.5 0.5 all-gather.18.cloned.1.call-update
  11.1 1.2 dynamic_slice.22
  12.3 1.3 dynamic_slice.19
  15.0 0.9 fusion.180
  15.9 1.8 copy.117
  18.4 0.6 iota_compare_fusion.1
  19.0 1.9 fusion.184
  20.9 2.0 fusion.183
  22.8 66.7 %all-gather.16.cloned.1.call-done = bf16[1,2048,512]{2,1,0:T(8,128)(2,1)} async-done(((bf16[1,32,512]{2,1,0:T(8,128)(2,1)}), bf16[1,2048,512]{2,1,0:T(8,128)(2,1)}) %all-gather.16.cloned.1.call-update) | async-done | bytes 2097168 | tf_op jit(solution)/shard_map/all_gather | solution.py:80
  89.5 2.9 fusion.178
  92.4 2.1 copy.97
  94.5 72.8 %all-gather.14.cloned.1.call-done = bf16[1,2048,512]{2,1,0:T(8,128)(2,1)} async-done(((bf16[1,32,512]{2,1,0:T(8,128)(2,1)}), bf16[1,2048,512]{2,1,0:T(8,128)(2,1)}) %all-gather.14.cloned.1.call-update) | async-done | bytes 2097168 | tf_op jit(solution)/shard_map/all_gather | solution.py:79
  167.2 2.9 fusion.179
  170.1 2.1 copy.118
  172.2 2.0 copy.120
  174.2 2.1 copy.119
  176.3 2.1 copy.121
  178.3 2.0 copy.93
  180.4 2.1 copy.89
  182.5 2.0 copy.85
  184.5 2.9 multiply_reduce_fusion
  187.4 1.7 multiply_reduce_fusion.2
  189.1 1.8 multiply_reduce_fusion.1
  190.9 2.3 multiply_reduce_fusion.3
  193.2 53.1 %all-gather.20.cloned.1.call-done = bf16[1,4096,512]{2,1,0:T(8,128)(2,1)} async-done(((bf16[1,64,512]{2,1,0:T(8,128)(2,1)}), bf16[1,4096,512]{2,1,0:T(8,128)(2,1)}) %all-gather.20.cloned.1.call-update) | async-done | bytes 4194320 | tf_op jit(solution)/shard_map/all_gather | solution.py:83
  246.3 78.8 %all-gather.18.cloned.1.call-done = bf16[1,4096,512]{2,1,0:T(8,128)(2,1)} async-done(((bf16[1,64,512]{2,1,0:T(8,128)(2,1)}), bf16[1,4096,512]{2,1,0:T(8,128)(2,1)}) %all-gather.18.cloned.1.call-update) | async-done | bytes 4194320 | tf_op jit(solution)/shard_map/all_gather | solution.py:82
  325.1 4.3 constant_dynamic-slice_fusion
  329.4 1.9 copy.122
  331.3 1.9 copy.98
  333.1 1.3 fusion.185
  334.5 0.7 fusion.176
  335.2 0.5 fusion.63
  335.7 0.4 convolution_bitcast_fusion.1
  336.1 0.2 fusion.61
  336.3 0.3 convolution_bitcast_fusion
  336.7 0.7 copy-done.1
  337.4 0.6 fusion.11
  338.0 0.2 copy-done.2
  338.2 0.6 fusion.9
  338.7 0.4 copy-done.3
  339.2 0.6 fusion.7
  339.7 0.2 copy-done.4
  339.9 0.6 fusion.5
  340.6 0.7 fusion.23
  341.2 0.3 copy-done.8
  341.5 0.7 fusion.21
  342.3 0.7 fusion.19
  343.0 0.3 copy-done.6
  343.3 0.7 fusion.25
  344.0 0.3 fusion.29
  344.3 1.7 convolution_convert_fusion
  346.1 0.5 all-gather.12.cloned.1.call-update
  346.6 0.3 reduce-scatter.2.cloned.1.call-start
  346.9 48.5 %all-gather.22.cloned.1.call-done = bf16[1024,2048]{1,0:T(8,128)(2,1)} async-done(((bf16[256,2048]{1,0:T(8,128)(2,1)}), bf16[1024,2048]{1,0:T(8,128)(2,1)}) %all-gather.22.cloned.1.call-update) | async-done | bytes 4194320 | tf_op jit(solution)/shard_map/all_gather | solution.py:107
  395.4 3.1 reduce_sum.121
  398.5 25.6 %all-gather.12.cloned.1.call-done = bf16[256,2048]{1,0:T(8,128)(2,1)} async-done(((bf16[256,512]{1,0:T(8,128)(2,1)}), bf16[256,2048]{1,0:T(8,128)(2,1)}) %all-gather.12.cloned.1.call-update) | async-done | bytes 1048592 | tf_op jit(solution)/shard_map/all_gather | solution.py:109
  424.1 2.5 convert_reduce_fusion
  426.6 9.5 %convolution_convert_fusion.1 = bf16[256,2048]{1,0:T(8,128)(2,1)} fusion(bf16[1024,2048]{1,0:T(8,128)(2,1)} %param.28, bf16[2048,1024]{1,0:T(8,128)(2,1)} %param.26, bf16[256,2048]{1,0:T(8,128)(2,1)} %get-tuple-element.7, f32[2048]{0:T(1024)S(1)} %copy-done.18, f32[2048]{0:T(1024)S(1)} %copy-done.19, f32[256]{0:T(256)S(1)} %get-tuple-element.38, ...), kind=kOutput, calls=%fused_computation.4 | convolution fusion | flops 2168455168 | bytes 10508288 | tf_op jit(solution)/shard_map/dot_general | solution.py:120
  436.1 0.8 dynamic_slice.23
  436.9 26.1 %reduce-scatter.2.cloned.1.call-done = bf16[256,512]{1,0:T(8,128)(2,1)} async-done(((bf16[256,2048]{1,0:T(8,128)(2,1)}), bf16[256,512]{1,0:T(8,128)(2,1)}) %reduce-scatter.2.cloned.1.call-update) | async-done | bytes 262160 | tf_op jit(solution)/shard_map/reduce_scatter | solution.py:121
  463.0 1.8 add_convert_fusion.1
  (52 shorter events, 0.6 us)
Async XLA Ops:
  6.5 337.7 %copy-start = (bf16[512,2048]{1,0:T(8,128)(2,1)S(1)}, bf16[512,2048]{1,0:T(8,128)(2,1)}, u32[]{:S(2)}) copy-start(bf16[512,2048]{1,0:T(8,128)(2,1)} %param.23) | copy-start | bytes 6291460
  6.5 14.3 %copy-start.5 = (bf16[256,512]{1,0:T(8,128)(2,1)S(1)}, bf16[256,512]{1,0:T(8,128)(2,1)}, u32[]{:S(2)}) copy-start(bf16[256,512]{1,0:T(8,128)(2,1)} %param.17) | copy-start | bytes 786436
  6.5 83.0 %all-gather.16.cloned.1.call-start = ((), (), s32[]{:S(2)}) async-start(), calls=%async_computation.4 | async-start | bytes 2129920 | tf_op jit(solution)/shard_map/all_gather | solution.py:80
  8.1 159.1 %all-gather.14.cloned.1.call-start = ((), (), s32[]{:S(2)}) async-start(), calls=%async_computation.3 | async-start | bytes 2129920 | tf_op jit(solution)/shard_map/all_gather | solution.py:79
  8.9 237.5 %all-gather.20.cloned.1.call-start = ((), (), s32[]{:S(2)}) async-start(), calls=%async_computation.6 | async-start | bytes 4259840 | tf_op jit(solution)/shard_map/all_gather | solution.py:83
  10.5 314.7 %all-gather.18.cloned.1.call-start = ((), (), s32[]{:S(2)}) async-start(), calls=%async_computation.5 | async-start | bytes 4259840 | tf_op jit(solution)/shard_map/all_gather | solution.py:82
  11.0 384.3 %all-gather.22.cloned.1.call-start = ((), (), s32[]{:S(2)}) async-start(), calls=%async_computation.7 | async-start | bytes 5242880 | tf_op jit(solution)/shard_map/all_gather | solution.py:107
  184.5 2.9 copy-start.12
  187.4 1.7 copy-start.11
  189.1 1.8 copy-start.10
  333.1 2.6 copy-start.15
  334.5 1.8 copy-start.13
  335.7 1.0 copy-start.14
  335.7 1.7 copy-start.1
  336.3 1.8 copy-start.2
  337.4 1.7 copy-start.3
  338.2 1.7 copy-start.4
  339.2 1.3 copy-start.16
  339.2 1.3 copy-start.17
  339.2 1.4 copy-start.9
  340.5 1.0 copy-start.8
  341.2 1.1 copy-start.7
  342.2 1.1 copy-start.6
  346.0 78.1 %all-gather.12.cloned.1.call-start = ((), (), s32[]{:S(2)}) async-start(), calls=%async_computation.1 | async-start | bytes 1310720 | tf_op jit(solution)/shard_map/all_gather | solution.py:109
  346.6 116.4 %reduce-scatter.2.cloned.1.call-start = ((), (), s32[]{:S(2)}) async-start(), calls=%async_computation.2 | async-start | bytes 1310720 | tf_op jit(solution)/shard_map/reduce_scatter | solution.py:121
  398.5 28.2 %copy-start.18 = (f32[2048]{0:T(1024)S(1)}, f32[2048]{0:T(1024)}, u32[]{:S(2)}) copy-start(f32[2048]{0:T(1024)} %param.25) | copy-start | bytes 24580
  398.5 28.2 %copy-start.19 = (f32[2048]{0:T(1024)S(1)}, f32[2048]{0:T(1024)}, u32[]{:S(2)}) copy-start(f32[2048]{0:T(1024)} %param.24) | copy-start | bytes 24580
  398.5 28.1 %copy-start.20 = (f32[1024]{0:T(1024)S(1)}, f32[1024]{0:T(1024)}, u32[]{:S(2)}) copy-start(f32[1024]{0:T(1024)} %param.27) | copy-start | bytes 12292
Sparse Core Ops, SparseCore 0:
  10.1 79.3 all-gather.15
  92.3 74.9 all-gather.13
  170.0 76.2 all-gather.19
  248.9 76.1 all-gather.17
  346.1 49.1 all-gather.21
  397.0 27.0 all-gather.11
  436.2 26.6 reduce-scatter.1
